TPU v7x, 32 devices: a whole 2x2x4 slice. The times are simulated.
32 devices in a mesh: seq: 8 (over z, y), fsdp: 4 (over x, core).
Axes of the slice: x: 2, y: 2, z: 4, core: 2. Of those that a mesh axis runs over, the one named last changes fastest.
Arguments:
- tokens: bfloat16 [2048, 2048], P('seq', 'fsdp'), may hold values from -6 to 6
- deal_order: int32 [8, 8], replicated, may hold values from 0 to 7, each once within a row
- lengths: int32 [4], replicated, may hold values from 1 to 1024, 2048 in all
- x_weight: bfloat16 [2048, 1536], P(None, 'fsdp'), may hold values from -0.0390625 to 0.0390625
- z_weight: bfloat16 [2048, 1536], P(None, 'fsdp'), may hold values from -0.125 to 0.125
- shared_weight: bfloat16 [2048, 512], P('fsdp'), may hold values from -0.0390625 to 0.0390625
- step_weight: bfloat16 [2048, 24], P(None, 'fsdp'), may hold values from -0.125 to 0.125
- conv_heads: float32 [4, 1536], P(None, 'fsdp'), may hold values from -3 to 3
- conv_shared: float32 [4, 512], replicated, may hold values from -3 to 3
- step_bias: float32 [24], P('fsdp'), as said below
- decay_log: float32 [24], P('fsdp'), may hold values from -7.1 to -2.8, as said below
- skip_gain: float32 [24], P('fsdp'), may hold values from 0.5 to 1.5
Outputs:
- mixed: bfloat16 [2048, 1536], P('seq', 'fsdp')
Inputs may be any that keep to these rules, and one draw needn't show every extreme that they name: `deal_order`: each row is a permutation of 0 to 7. The lengths sum to 2048. `decay_log`: one value a head. `step_bias`: one value a head.
All inputs are finite; a program needn't handle non-finite values.
Results may differ from a plain program's by a relative error of at most 0.0095.
Values may be sent and summed in bfloat16 or wider, within the bound.
No kernel may reach another device: no remote copies, remote signals or barrier semaphores. Data moves between devices by JAX's collectives and lax.ppermute only.
A program may use at most 128 MiB of HBM per device.

v0:
```python
import jax
import jax.numpy as jnp
from jax import lax
from jax.sharding import PartitionSpec as P

precise = lax.Precision.HIGHEST


def shifted(array, axis, by):
    count = lax.axis_size(axis)
    pairs = [(i, i + by) for i in range(count) if 0 <= i + by < count]
    return lax.ppermute(array, axis, pairs)


def prefix(part, axis, combine, identity):
    place = lax.axis_index(axis)
    gathered = jax.tree.map(lambda a: lax.all_gather(a, axis), part)
    state = jax.tree.map(lambda a, e: jnp.zeros_like(a) + jnp.asarray(e, a.dtype), part, identity)

    def one(turn, state):
        return combine(
            state, jax.tree.map(lambda a: lax.dynamic_index_in_dim(a, turn, 0, False), gathered)
        )

    return lax.fori_loop(0, place, one, state)


def segment_of(positions, lengths):
    prompt_ends = jnp.cumsum(lengths)
    counted = (positions[:, None] >= prompt_ends[None, :]).astype(jnp.int32)
    return jnp.sum(counted, axis=1)


def causal_conv(extended, segment_ids, weights, conv_width):
    out_rows = extended.shape[0] - conv_width + 1
    target = segment_ids[conv_width - 1 :]
    running = jnp.zeros((out_rows, extended.shape[1]), jnp.float32)
    for tap_index in range(conv_width):
        matched = (segment_ids[tap_index : tap_index + out_rows] == target).astype(jnp.float32)
        running = (
            running
            + weights[tap_index][None, :]
            * extended[tap_index : tap_index + out_rows]
            * matched[:, None]
        )
    return running


def local_terms(x_heads, b_rows, c_rows, step_size, decay_log, segment_ids, seg_before):
    log_decay = -jnp.exp(decay_log)[None, :] * step_size
    cum_decay = jnp.cumsum(log_decay, axis=0)
    positions_in = jnp.arange(x_heads.shape[0], dtype=jnp.int32)
    same_prompt = (segment_ids[:, None] == segment_ids[None, :]) & (
        positions_in[:, None] >= positions_in[None, :]
    )
    decay_gap = cum_decay.T[:, :, None] - cum_decay.T[:, None, :]
    decay_matrix = jnp.exp(jnp.where(same_prompt[None], decay_gap, -jnp.inf))
    scores = jnp.dot(c_rows, b_rows.T, precision=precise)
    x_step = x_heads * step_size[:, :, None]
    intra = jnp.einsum("hts,shp->thp", scores[None] * decay_matrix, x_step, precision=precise)
    to_end = jnp.exp(
        jnp.where(
            (segment_ids == segment_ids[-1])[:, None], cum_decay[-1][None, :] - cum_decay, -jnp.inf
        )
    )
    state_out = jnp.einsum("shp,sn->hpn", x_step * to_end[:, :, None], b_rows, precision=precise)
    carried = segment_ids == seg_before
    carry_in = jnp.exp(jnp.where(carried[:, None], cum_decay, -jnp.inf))
    block_decay = jnp.where(carried[-1], jnp.exp(cum_decay[-1]), 0.0)
    return (intra, state_out, carry_in, block_decay)


def combine(earlier, later):
    return (earlier[0] * later[0], later[0][:, None, None] * earlier[1] + later[1])


def per_device(
    tokens,
    deal_order,
    lengths,
    x_weight,
    z_weight,
    shared_weight,
    step_weight,
    conv_heads,
    conv_shared,
    step_bias,
    decay_log,
    skip_gain,
):
    seq_count = lax.axis_size("seq")
    own_index = lax.axis_index("seq")
    tok_dev = tokens.shape[0]
    piece_rows = tok_dev // seq_count
    slot_rows = tokens.reshape(seq_count, piece_rows, tokens.shape[1])
    arrived = lax.all_to_all(slot_rows, "seq", split_axis=0, concat_axis=0, tiled=True)
    dealt_row = lax.dynamic_slice_in_dim(deal_order, own_index, 1, 0)[0]
    inverse = jnp.argsort(dealt_row)
    stream_block = jnp.take(arrived, inverse, axis=0).reshape(tok_dev, tokens.shape[1])
    inner_dev = x_weight.shape[1]
    heads_dev = step_weight.shape[1]
    head_dim = inner_dev // heads_dev
    state_dim = shared_weight.shape[1] // 2
    w_full = lax.all_gather(shared_weight, "fsdp", axis=0, tiled=True)
    weight_list = (x_weight, z_weight, step_weight, w_full)
    feature_part = lax.all_gather(stream_block, "fsdp", axis=1, tiled=True)
    x_acc, z_acc, step_acc, bc_acc = tuple(
        (
            jnp.dot(feature_part, weight, preferred_element_type=jnp.float32)
            for weight in weight_list
        )
    )
    x_raw = x_acc.astype(jnp.bfloat16)
    z_raw = z_acc.astype(jnp.bfloat16)
    bc_raw = bc_acc.astype(jnp.bfloat16)
    step_size = jax.nn.softplus(step_acc + step_bias[None, :])
    mixed_in = jnp.concatenate([x_raw, bc_raw], axis=1)
    conv_width = conv_heads.shape[0]
    prior_rows = shifted(mixed_in[tok_dev - conv_width + 1 :], "seq", 1)
    first_pos = own_index * tok_dev
    positions = first_pos - (conv_width - 1) + jnp.arange(tok_dev + conv_width - 1, dtype=jnp.int32)
    seg_ext = segment_of(positions, lengths)
    extended = jnp.concatenate([prior_rows, mixed_in], axis=0).astype(jnp.float32)
    activated = jax.nn.silu(
        causal_conv(
            extended, seg_ext, jnp.concatenate([conv_heads, conv_shared], axis=1), conv_width
        )
    )
    segment_ids = seg_ext[conv_width - 1 :]
    seg_before = jnp.where(own_index == 0, -1, seg_ext[conv_width - 2])
    x_heads = activated[:, :inner_dev].reshape(tok_dev, heads_dev, head_dim)
    b_rows = activated[:, inner_dev : inner_dev + state_dim]
    c_rows = activated[:, inner_dev + state_dim :]
    intra, state_out, carry_in, block_decay = local_terms(
        x_heads, b_rows, c_rows, step_size, decay_log, segment_ids, seg_before
    )
    identity = (jnp.ones_like(block_decay), jnp.zeros_like(state_out))
    _, state_in = prefix((block_decay, state_out), "seq", combine, identity)
    incoming = jnp.einsum("tn,hpn->thp", c_rows, state_in, precision=precise)
    y_block = intra + carry_in[:, :, None] * incoming + skip_gain[None, :, None] * x_heads
    gated = (y_block.reshape(tok_dev, inner_dev) * jax.nn.silu(z_raw.astype(jnp.float32))).astype(
        jnp.bfloat16
    )
    ordered = gated.reshape(seq_count, piece_rows, inner_dev)
    outgoing = jnp.take(ordered, dealt_row, axis=0)
    returned = lax.all_to_all(outgoing, "seq", split_axis=0, concat_axis=0, tiled=True)
    return returned.reshape(tok_dev, inner_dev)


def solution(mesh):
    return jax.shard_map(
        per_device,
        mesh=mesh,
        in_specs=(
            P("seq", "fsdp"),
            P(),
            P(),
            P(None, "fsdp"),
            P(None, "fsdp"),
            P("fsdp", None),
            P(None, "fsdp"),
            P(None, "fsdp"),
            P(),
            P("fsdp"),
            P("fsdp"),
            P("fsdp"),
        ),
        out_specs=P("seq", "fsdp"),
        check_vma=False,
    )
```

profile of v0, /device:TPU:0, one launch (start us, length us, event | category | flops | bytes accessed | tf_op | source)
XLA Modules:
  0.0 173.2 jit_solution(6664324433288918847)
XLA Ops:
  6.5 0.0 copy-start
  6.5 0.0 copy-start.2
  6.6 0.0 copy-start.7
  6.6 7.4 %all-to-all-start = ((bf16[8,32,512]{2,1,0:T(8,128)(2,1)}), bf16[8,32,512]{2,1,0:T(8,128)(2,1)S(1)}, u32[]{:S(2)}, u32[]{:S(2)}) async-start(bf16[8,32,512]{2,1,0:T(8,128)(2,1)} %bitcast.90), calls=%async_computation | async-start | bytes 524288 | tf_op jit(solution)/shard_map/all_to_all | solution.py:96
  14.0 0.0 all-gather.6.cloned.1.call-start
  14.0 1.3 compare_and_fusion.1
  15.3 1.0 sort.17
  16.3 0.1 broadcast_in_dim.88
  16.4 0.1 broadcast_in_dim.89
  16.5 6.5 %all-to-all-done = bf16[8,32,512]{2,1,0:T(8,128)(2,1)S(1)} async-done(((bf16[8,32,512]{2,1,0:T(8,128)(2,1)}), bf16[8,32,512]{2,1,0:T(8,128)(2,1)S(1)}, u32[]{:S(2)}, u32[]{:S(2)}) %all-to-all-start) | async-done | bytes 262176 | tf_op jit(solution)/shard_map/all_to_all | solution.py:96
  22.9 0.6 gather_fusion
  23.5 0.8 bitcast_select_fusion
  24.3 0.0 all-gather.6.cloned.1.call-update
  24.3 0.0 all-gather.8.cloned.1.call-start
  24.4 0.7 all-gather.8.cloned.1.call-update
  25.1 0.0 all-gather.10.cloned.1.call-start
  25.1 0.0 copy-done.8
  25.2 0.2 reduce-window.18
  25.3 0.1 convert_reduce_fusion
  25.4 0.6 fusion.51
  26.6 0.7 broadcast_compare_fusion
  27.4 0.6 slice.89
  28.0 0.0 copy-done.5
  28.0 0.0 copy-done.4
  28.0 0.0 copy-done.9
  28.0 12.2 %all-gather.6.cloned.1.call-done = bf16[256,2048]{1,0:T(8,128)(2,1)} async-done(((bf16[256,512]{1,0:T(8,128)(2,1)}), bf16[256,2048]{1,0:T(8,128)(2,1)}) %all-gather.6.cloned.1.call-update) | async-done | bytes 1048592 | tf_op jit(solution)/shard_map/all_gather | solution.py:106
  40.3 0.0 copy-done.2
  40.3 0.0 copy-done.7
  40.3 1.6 fusion.41
  41.9 0.0 copy-start.1
  41.9 1.8 %reduce-window.19 = f32[6,2,128]{2,1,0:T(2,128)S(1)} reduce-window(f32[6,2,128]{2,1,0:T(2,128)S(1)} %reshape.175, f32[]{:T(128)} %constant.76.clone.1), window={size=1x1x128 pad=0_0x0_0x127_0}, to_apply=%region_3.4 | reduce-window | flops 195072 | bytes 12292 | tf_op jit(solution)/shard_map/reduce-window.1
  43.8 0.1 slice.107
  43.8 0.1 copy.47
  44.0 0.1 copy.48
  44.1 0.1 add_bitcast_fusion
  44.2 0.8 slice_reduce_fusion
  45.0 0.0 copy-done.3
  45.0 0.1 select_exponential_fusion.1
  45.1 1.9 %convolution_convert_fusion.2 = bf16[256,384]{1,0:T(8,128)(2,1)S(1)} fusion(bf16[256,2048]{1,0:T(8,128)(2,1)} %all-gather.6.cloned.1.call-done, bf16[2048,384]{1,0:T(8,128)(2,1)S(1)} %copy-done), kind=kOutput, calls=%fused_computation.16 | convolution fusion | flops 402751488 | bytes 2818048 | tf_op jit(solution)/shard_map/dot_general | solution.py:109
  47.0 17.4 %all-gather.8.cloned.1.call-done = bf16[2048,512]{1,0:T(8,128)(2,1)} async-done(((bf16[512,512]{1,0:T(8,128)(2,1)}), bf16[2048,512]{1,0:T(8,128)(2,1)}) %all-gather.8.cloned.1.call-update) | async-done | bytes 2097168 | tf_op jit(solution)/shard_map/all_gather | solution.py:104
  64.5 0.0 copy-done.1
  64.5 2.3 %convolution_convert_fusion = bf16[256,512]{1,0:T(8,128)(2,1)S(1)} fusion(bf16[256,2048]{1,0:T(8,128)(2,1)S(1)} %copy-done.1, bf16[2048,512]{1,0:T(8,128)(2,1)} %all-gather.8.cloned.1.call-done), kind=kOutput, calls=%fused_computation.12 | convolution fusion | flops 537001984 | bytes 3407872 | tf_op jit(solution)/shard_map/dot_general | solution.py:109
  66.8 3.4 %collective-permute-start = (bf16[3,896]{1,0:T(4,128)(2,1)S(1)}, bf16[3,896]{1,0:T(4,128)(2,1)S(1)}, u32[]{:S(2)}, u32[]{:S(2)}) collective-permute-start(bf16[3,896]{1,0:T(4,128)(2,1)S(1)} %pad_maximum_fusion), channel_id=1, source_target_pairs={{0,4},{4,8},{8,12},{12,16},{16,20},{20,24},{24,28},{1,5},{5,9},{9,... | collective-permute-start | bytes 16136 | tf_op jit(solution)/shard_map/ppermute | solution.py:12
  70.2 1.3 collective-permute-done
  71.5 0.1 maximum_convert_fusion
  71.6 0.7 divide_multiply_fusion
  72.3 0.2 copy.46
  72.5 1.2 fusion.26
  73.7 0.0 all-gather.10.cloned.1.call-update
  73.8 0.1 slice.74
  73.8 0.7 fusion.47
  74.5 0.6 pad_clamp_fusion
  75.1 0.7 fusion.32
  75.9 21.6 %all-gather.1 = f32[8,1,6]{2,1,0:T(1,128)} all-gather(f32[1,1,6]{2,1,0:T(1,128)S(1)} %bitcast.96), channel_id=1, replica_groups=mesh['seq'=8,'fsdp'=4] {'seq'}, dimensions={0}, use_global_device_ids=true | all-gather | bytes 216 | tf_op jit(solution)/shard_map/all_gather | solution.py:17
  97.5 0.4 fusion.34
  97.9 37.2 %all-gather.10.cloned.1.call-done = f32[48,64,256]{2,1,0:T(8,128)} async-done(((f32[6,64,256]{2,1,0:T(8,128)}), f32[48,64,256]{2,1,0:T(8,128)}) %all-gather.10.cloned.1.call-update) | async-done | bytes 3145744 | tf_op jit(solution)/shard_map/all_gather | solution.py:17
  135.2 0.5 convolution_multiply_fusion
  135.7 2.8 %fusion.11 = f32[256,6,64]{0,2,1:T(8,128)S(1)} fusion(f32[256,6,64]{0,2,1:T(8,128)S(1)} %convolution_multiply_fusion, f32[6,256]{1,0:T(8,128)} %bitcast.93, f32[256,256]{1,0:T(8,128)S(1)} %fusion.34, pred[256,256]{1,0:T(8,128)(4,1)} %fusion.32, f32[256,6,64]{0,2,1:T(8,128)S(1)} %bitcast.86, f32[6]{0:T(128)} %param.25, f32[256,6]{0,1:T(8,128)S(1)} %compare_select_fusion.1), kind=kOutput, calls=%fused_computation.11 | convolution fusion | flops 303562752 | bytes 1519640 | tf_op jit(solution)/shard_map/hts,shp->thp/dot_general | solution.py:60
  138.5 0.2 copy.49
  138.7 2.5 %multiply_convert_fusion = bf16[256,384]{1,0:T(8,128)(2,1)S(1)} fusion(f32[256,384]{1,0:T(8,128)S(1)} %copy.49, bf16[256,2048]{1,0:T(8,128)(2,1)} %all-gather.6.cloned.1.call-done, bf16[2048,384]{1,0:T(8,128)(2,1)} %param.18), kind=kOutput, calls=%fused_computation.35 | convolution fusion | flops 403439616 | bytes 3211264 | tf_op jit(solution)/shard_map/dot_general | solution.py:109
  141.2 0.7 gather_fusion.1
  141.9 0.1 broadcast_select_fusion
  142.0 24.0 %all_to_all.10 = bf16[8,32,384]{2,1,0:T(8,128)(2,1)S(1)} all-to-all(bf16[8,32,384]{2,1,0:T(8,128)(2,1)S(1)} %broadcast_select_fusion), channel_id=1, replica_groups=mesh['seq'=8,'fsdp'=4] {'seq'}, dimensions={0} | all-to-all | bytes 393216 | tf_op jit(solution)/shard_map/all_to_all | solution.py:146
  166.0 0.7 copy.67
  (26 shorter events, 0.2 us)
Async XLA Ops:
  6.5 38.6 %copy-start = (bf16[2048,384]{1,0:T(8,128)(2,1)S(1)}, bf16[2048,384]{1,0:T(8,128)(2,1)}, u32[]{:S(2)}) copy-start(bf16[2048,384]{1,0:T(8,128)(2,1)} %param.17) | copy-start | bytes 4718596
  6.5 18.6 %copy-start.8 = (s32[4]{0:T(128)S(1)}, s32[4]{0:T(128)}, u32[]{:S(2)}) copy-start(s32[4]{0:T(128)} %param.16) | copy-start | bytes 52
  6.5 21.4 %copy-start.5 = (f32[4,384]{1,0:T(4,128)S(1)}, f32[4,384]{1,0:T(4,128)}, u32[]{:S(2)}) copy-start(f32[4,384]{1,0:T(4,128)} %param.21) | copy-start | bytes 18436
  6.5 21.4 %copy-start.4 = (f32[4,512]{1,0:T(4,128)S(1)}, f32[4,512]{1,0:T(4,128)}, u32[]{:S(2)}) copy-start(f32[4,512]{1,0:T(4,128)} %param.22) | copy-start | bytes 24580
  6.5 21.5 %copy-start.9 = (f32[6]{0:T(128)S(1)}, f32[6]{0:T(128)}, u32[]{:S(2)}) copy-start(f32[6]{0:T(128)} %param.24) | copy-start | bytes 76
  6.5 33.7 %copy-start.2 = (bf16[2048,6]{0,1:T(8,128)(2,1)S(1)}, bf16[2048,6]{0,1:T(8,128)(2,1)}, u32[]{:S(2)}) copy-start(bf16[2048,6]{0,1:T(8,128)(2,1)} %param.20) | copy-start | bytes 73732
  6.6 33.7 %copy-start.7 = (f32[6]{0:T(128)S(1)}, f32[6]{0:T(128)}, u32[]{:S(2)}) copy-start(f32[6]{0:T(128)} %param.23) | copy-start | bytes 76
  6.6 16.3 %all-to-all-start = ((bf16[8,32,512]{2,1,0:T(8,128)(2,1)}), bf16[8,32,512]{2,1,0:T(8,128)(2,1)S(1)}, u32[]{:S(2)}, u32[]{:S(2)}) async-start(bf16[8,32,512]{2,1,0:T(8,128)(2,1)} %bitcast.90), calls=%async_computation | async-start | bytes 524288 | tf_op jit(solution)/shard_map/all_to_all | solution.py:96
  14.0 26.3 %all-gather.6.cloned.1.call-start = ((), (), s32[]{:S(2)}) async-start(), calls=%async_computation.2 | async-start | bytes 1310720 | tf_op jit(solution)/shard_map/all_gather | solution.py:106
  24.3 40.1 %all-gather.8.cloned.1.call-start = ((), (), s32[]{:S(2)}) async-start(), calls=%async_computation.3 | async-start | bytes 2621440 | tf_op jit(solution)/shard_map/all_gather | solution.py:104
  25.1 110.1 %all-gather.10.cloned.1.call-start = ((), (), s32[]{:S(2)}) async-start(), calls=%async_computation.4 | async-start | bytes 3538944 | tf_op jit(solution)/shard_map/all_gather | solution.py:17
  41.9 22.5 %copy-start.1 = (bf16[256,2048]{1,0:T(8,128)(2,1)S(1)}, bf16[256,2048]{1,0:T(8,128)(2,1)}, u32[]{:S(2)}) copy-start(bf16[256,2048]{1,0:T(8,128)(2,1)} %all-gather.6.cloned.1.call-done) | copy-start | bytes 3145732
  44.2 0.8 copy-start.3
  66.8 4.7 %collective-permute-start = (bf16[3,896]{1,0:T(4,128)(2,1)S(1)}, bf16[3,896]{1,0:T(4,128)(2,1)S(1)}, u32[]{:S(2)}, u32[]{:S(2)}) collective-permute-start(bf16[3,896]{1,0:T(4,128)(2,1)S(1)} %pad_maximum_fusion), channel_id=1, source_target_pairs={{0,4},{4,8},{8,12},{12,16},{16,20},{20,24},{24,28},{1,5},{5,9},{9,... | collective-permute-start | bytes 16136 | tf_op jit(solution)/shard_map/ppermute | solution.py:12
  138.7 3.2 %copy-start.6 = (pred[8]{0:T(512)(128)(4,1)S(1)}, pred[8]{0:T(512)(128)(4,1)}, u32[]{:S(2)}) copy-start(pred[8]{0:T(512)(128)(4,1)} %get-tuple-element.68) | copy-start | bytes 28
Sparse Core Ops, SparseCore 0:
  24.5 15.7 all-gather.5
  41.8 22.5 all-gather.7
  73.9 61.2 all-gather.9
where the time goes:
time: 174 us; the launch traced here: 173 us
  waiting for transfers between devices  75.4 us (43%)
  blocking collectives  45.7 us (26%)
  between operations  14 us (8%)
  matrix products  13.3 us (8%)
  starting transfers between devices  10.9 us (6%)
  other arithmetic  9.84 us (6%)
  local copies, waits for them, and re-layouts  4.14 us (2%)
    all_gather x1, waiting for transfers between devices, prefix(): gathered = jax.tree.map(lambda a: lax.all_gather(a, axis), part)  37.2 us
    all_to_all x1, blocking collectives, per_device(): lax.all_to_all(outgoing, 'seq', split_axis=0, concat_axis=0, tiled=True)  24 us
    all_gather x1, blocking collectives, prefix(): gathered = jax.tree.map(lambda a: lax.all_gather(a, axis), part)  21.6 us
    all_gather x1, waiting for transfers between devices, per_device(): w_full = lax.all_gather(shared_weight, 'fsdp', axis=0, tiled=True)  17.4 us
    all_gather x1, waiting for transfers between devices, per_device(): feature_part = lax.all_gather(stream_block, 'fsdp', axis=1, tiled=True)  12.2 us
    dot_general x4, matrix products, per_device(): jnp.dot(feature_part, weight, preferred_element_type=jnp.float32)  8.34 us
    all_to_all x1, starting transfers between devices, per_device(): lax.all_to_all(slot_rows, 'seq', split_axis=0, concat_axis=0, tiled=True)  7.42 us
    all_to_all x1, waiting for transfers between devices, per_device(): lax.all_to_all(slot_rows, 'seq', split_axis=0, concat_axis=0, tiled=True)  6.45 us
  transfers between devices with their start and end apart: 5, of which 5 were waited for; matrix products, arithmetic and copies ran while one was open for 8% of the time, Pallas kernels for 0%

commit v1 on v0

--- a/solution.py
+++ b/solution.py
@@ -4,6 +4,17 @@
 from jax.sharding import PartitionSpec as P
 
 precise = lax.Precision.HIGHEST
+
+
+def around_the_ring(x, name, d):
+    count = lax.axis_size(name)
+    right = [(i, (i + 1) % count) for i in range(count)]
+    parts = [x]
+    for far in range(1, count):
+        parts = [lax.ppermute(parts[0], name, right), *parts]
+    full = jnp.concatenate(parts, axis=d)
+    offset = (lax.axis_index(name) + 1) * parts[-1].shape[d]
+    return jnp.roll(full, offset, axis=d)
 
 
 def shifted(array, axis, by):
@@ -101,7 +112,7 @@
     heads_dev = step_weight.shape[1]
     head_dim = inner_dev // heads_dev
     state_dim = shared_weight.shape[1] // 2
-    w_full = lax.all_gather(shared_weight, "fsdp", axis=0, tiled=True)
+    w_full = around_the_ring(shared_weight, "fsdp", 0)
     weight_list = (x_weight, z_weight, step_weight, w_full)
     feature_part = lax.all_gather(stream_block, "fsdp", axis=1, tiled=True)
     x_acc, z_acc, step_acc, bc_acc = tuple(

time: 174 us -> 167 us (0.960)
  waiting for transfers between devices: 75.4 us -> 59.6 us
  local copies, waits for them, and re-layouts: 4.14 us -> 13.2 us
  blocking collectives: 45.7 us -> 43.6 us
    ppermute x0 -> x3, waiting for transfers between devices: none -> 21.2 us  [around_the_ring(): parts = [lax.ppermute(parts[0], name, right), *parts]]
    all_gather x1 -> x0, waiting for transfers between devices: 17.4 us -> none  [per_device(): w_full = lax.all_gather(shared_weight, 'fsdp', axis=0, tiled=True)]
    all_gather x1, waiting for transfers between devices: 12.2 us -> 0.01 us  [per_device(): feature_part = lax.all_gather(stream_block, 'fsdp', axis=1, tiled=True)]
    unnamed x23 -> x24, local copies, waits for them, and re-layouts: 0.72 us -> 7.27 us
    all_to_all x1, waiting for transfers between devices: 6.45 us -> 0.1 us  [per_device(): lax.all_to_all(slot_rows, 'seq', split_axis=0, concat_axis=0, tiled=True)]
    all_gather x1, blocking collectives: 21.6 us -> 19.7 us  [prefix(): gathered = jax.tree.map(lambda a: lax.all_gather(a, axis), part)]
  transfers between devices with their start and end apart: 5 -> 7, of which waited for: 5 -> 5; matrix products, arithmetic and copies ran while one was open for 8% -> 14% of each run, Pallas kernels for 0% -> 0%
where the time goes in v1:
time: 167 us; the launch traced here: 166 us
  waiting for transfers between devices  59.6 us (36%)
  blocking collectives  43.6 us (26%)
  between operations  14.3 us (9%)
  local copies, waits for them, and re-layouts  13.2 us (8%)
  matrix products  12.4 us (7%)
  starting transfers between devices  11.4 us (7%)
  other arithmetic  11 us (7%)
    all_gather x1, waiting for transfers between devices, prefix(): gathered = jax.tree.map(lambda a: lax.all_gather(a, axis), part)  38.3 us
    all_to_all x1, blocking collectives, per_device(): lax.all_to_all(outgoing, 'seq', split_axis=0, concat_axis=0, tiled=True)  23.9 us
    ppermute x3, waiting for transfers between devices, around_the_ring(): parts = [lax.ppermute(parts[0], name, right), *parts]  21.2 us
    all_gather x1, blocking collectives, prefix(): gathered = jax.tree.map(lambda a: lax.all_gather(a, axis), part)  19.7 us
    dot_general x4, matrix products, per_device(): jnp.dot(feature_part, weight, preferred_element_type=jnp.float32)  7.53 us
    all_to_all x1, starting transfers between devices, per_device(): lax.all_to_all(slot_rows, 'seq', split_axis=0, concat_axis=0, tiled=True)  7.41 us
    unnamed x24, local copies, waits for them, and re-layouts  7.27 us
    ppermute x1, starting transfers between devices, shifted(): return lax.ppermute(array, axis, pairs)  3.83 us
  transfers between devices with their start and end apart: 7, of which 5 were waited for; matrix products, arithmetic and copies ran while one was open for 14% of the time, Pallas kernels for 0%

profile of v1, /device:TPU:0, one launch (start us, length us, event | category | flops | bytes accessed | tf_op | source)
XLA Modules:
  0.0 165.7 jit_solution(7249064183280385666)
XLA Ops:
  6.5 7.4 %all-to-all-start = ((bf16[8,32,512]{2,1,0:T(8,128)(2,1)}), bf16[8,32,512]{2,1,0:T(8,128)(2,1)}, u32[]{:S(2)}, u32[]{:S(2)}) async-start(bf16[8,32,512]{2,1,0:T(8,128)(2,1)} %bitcast.89), calls=%async_computation | async-start | bytes 524288 | tf_op jit(solution)/shard_map/all_to_all | solution.py:107
  14.0 0.0 all-gather.5.cloned.1.call-start
  14.0 0.1 collective-permute-start
  14.1 1.2 compare_and_fusion.1
  15.2 1.0 sort.17
  16.2 0.8 reduce-window.18
  17.1 0.1 convert_reduce_fusion
  17.1 0.1 broadcast_in_dim.88
  17.2 0.1 broadcast_in_dim.89
  17.3 0.6 fusion.57
  18.6 4.3 %collective-permute-done = bf16[512,512]{1,0:T(8,128)(2,1)S(1)} collective-permute-done((bf16[512,512]{1,0:T(8,128)(2,1)}, bf16[512,512]{1,0:T(8,128)(2,1)S(1)}, u32[]{:S(2)}, u32[]{:S(2)}) %collective-permute-start) | collective-permute-done | bytes 524320 | tf_op jit(solution)/shard_map/ppermute | solution.py:14
  22.9 0.0 collective-permute-start.1
  22.9 0.1 all-to-all-done
  23.0 1.5 gather_fusion
  24.5 0.8 bitcast_select_fusion
  25.3 0.0 all-gather.5.cloned.1.call-update
  25.3 0.0 all-gather.7.cloned.1.call-start
  25.4 0.7 broadcast_compare_fusion
  26.1 0.6 slice.89
  26.7 4.8 %collective-permute-done.1 = bf16[512,512]{1,0:T(8,128)(2,1)S(1)} collective-permute-done((bf16[512,512]{1,0:T(8,128)(2,1)S(1)}, bf16[512,512]{1,0:T(8,128)(2,1)S(1)}, u32[]{:S(2)}, u32[]{:S(2)}) %collective-permute-start.1) | collective-permute-done | bytes 524320 | tf_op jit(solution)/shard_map/ppermute | solution.py:14
  31.5 0.0 collective-permute-start.2
  31.5 0.7 constant_dynamic-update-slice_fusion.1
  32.2 0.7 constant_dynamic-update-slice_fusion
  32.9 0.7 exponential_negate_fusion
  33.6 12.1 %collective-permute-done.2 = bf16[512,512]{1,0:T(8,128)(2,1)S(1)} collective-permute-done((bf16[512,512]{1,0:T(8,128)(2,1)S(1)}, bf16[512,512]{1,0:T(8,128)(2,1)S(1)}, u32[]{:S(2)}, u32[]{:S(2)}) %collective-permute-start.2) | collective-permute-done | bytes 524320 | tf_op jit(solution)/shard_map/ppermute | solution.py:14
  45.7 0.8 constant_dynamic-update-slice_fusion.9
  46.5 0.8 constant_dynamic-update-slice_fusion.8
  47.4 0.9 constant_dynamic-update-slice_fusion.7
  48.2 0.8 constant_dynamic-update-slice_fusion.6
  49.1 0.8 constant_dynamic-update-slice_fusion.5
  49.9 0.8 constant_dynamic-update-slice_fusion.4
  50.7 0.8 constant_dynamic-update-slice_fusion.3
  51.6 0.8 constant_dynamic-update-slice_fusion.2
  52.4 2.0 %convolution_convert_fusion.1 = bf16[256,384]{1,0:T(8,128)(2,1)S(1)} fusion(bf16[256,2048]{1,0:T(8,128)(2,1)} %all-gather.5.cloned.1.call-done, bf16[2048,384]{1,0:T(8,128)(2,1)S(1)} %copy-done), kind=kOutput, calls=%fused_computation.18 | convolution fusion | flops 402751488 | bytes 2818048 | tf_op jit(solution)/shard_map/dot_general | solution.py:120
  54.4 2.6 %fusion.16 = bf16[256,512]{1,0:T(8,128)(2,1)S(1)} fusion(bf16[256,2048]{1,0:T(8,128)(2,1)} %all-gather.5.cloned.1.call-done, bf16[4096,512]{1,0:T(8,128)(2,1)} %constant_dynamic-update-slice_fusion.2, s32[]{:T(128)S(6)} %select_n.88), kind=kOutput, calls=%fused_computation.14 | convolution fusion | flops 537001984 | bytes 3407876 | tf_op jit(solution)/shard_map/dot_general | solution.py:120
  57.1 3.8 %collective-permute-start.3 = (bf16[3,896]{1,0:T(4,128)(2,1)S(1)}, bf16[3,896]{1,0:T(4,128)(2,1)S(1)}, u32[]{:S(2)}, u32[]{:S(2)}) collective-permute-start(bf16[3,896]{1,0:T(4,128)(2,1)S(1)} %pad_maximum_fusion), channel_id=1, source_target_pairs={{0,4},{4,8},{8,12},{12,16},{16,20},{20,24},{24,28},{1,5},{5,9},{9,... | collective-permute-start | bytes 16136 | tf_op jit(solution)/shard_map/ppermute | solution.py:23
  61.0 0.4 fusion.46
  61.4 1.8 %reduce-window.19 = f32[6,2,128]{2,1,0:T(2,128)S(1)} reduce-window(f32[6,2,128]{2,1,0:T(2,128)S(1)} %reshape.175, f32[]{:T(128)} %constant.104.clone.1), window={size=1x1x128 pad=0_0x0_0x127_0}, to_apply=%region_3.4 | reduce-window | flops 195072 | bytes 12292 | tf_op jit(solution)/shard_map/reduce-window.1
  63.2 0.1 slice.107
  63.3 0.1 copy.47
  63.4 0.1 copy.48
  63.5 0.1 add_bitcast_fusion
  63.6 0.8 slice_reduce_fusion
  64.5 0.1 select_exponential_fusion.1
  64.6 0.1 maximum_convert_fusion
  64.7 0.7 divide_multiply_fusion
  65.4 0.2 copy.46
  65.6 1.2 fusion.31
  66.8 0.0 all-gather.7.cloned.1.call-update
  66.8 0.1 slice.74
  66.9 0.7 fusion.52
  67.6 0.6 pad_clamp_fusion
  68.2 0.7 fusion.37
  68.9 19.7 %all-gather.1 = f32[8,1,6]{2,1,0:T(1,128)} all-gather(f32[1,1,6]{2,1,0:T(1,128)S(1)} %bitcast.95), channel_id=1, replica_groups=mesh['seq'=8,'fsdp'=4] {'seq'}, dimensions={0}, use_global_device_ids=true | all-gather | bytes 216 | tf_op jit(solution)/shard_map/all_gather | solution.py:28
  88.7 0.4 fusion.39
  89.1 38.3 %all-gather.7.cloned.1.call-done = f32[48,64,256]{2,1,0:T(8,128)} async-done(((f32[6,64,256]{2,1,0:T(8,128)}), f32[48,64,256]{2,1,0:T(8,128)}) %all-gather.7.cloned.1.call-update) | async-done | bytes 3145744 | tf_op jit(solution)/shard_map/all_gather | solution.py:28
  127.5 0.5 convolution_multiply_fusion
  128.0 2.8 %fusion.13 = f32[256,6,64]{0,2,1:T(8,128)S(1)} fusion(f32[256,6,64]{0,2,1:T(8,128)S(1)} %convolution_multiply_fusion, f32[6,256]{1,0:T(8,128)} %bitcast.92, f32[256,256]{1,0:T(8,128)S(1)} %fusion.39, pred[256,256]{1,0:T(8,128)(4,1)} %fusion.37, f32[256,6,64]{0,2,1:T(8,128)S(1)} %bitcast.85, f32[6]{0:T(128)} %param.25, f32[256,6]{0,1:T(8,128)S(1)} %compare_select_fusion.1), kind=kOutput, calls=%fused_computation.13 | convolution fusion | flops 303562752 | bytes 1519640 | tf_op jit(solution)/shard_map/hts,shp->thp/dot_general | solution.py:71
  130.8 0.2 copy.49
  130.9 2.5 %multiply_convert_fusion = bf16[256,384]{1,0:T(8,128)(2,1)S(1)} fusion(f32[256,384]{1,0:T(8,128)S(1)} %copy.49, bf16[256,2048]{1,0:T(8,128)(2,1)} %all-gather.5.cloned.1.call-done, bf16[2048,384]{1,0:T(8,128)(2,1)} %param.18), kind=kOutput, calls=%fused_computation.37 | convolution fusion | flops 403439616 | bytes 3211264 | tf_op jit(solution)/shard_map/dot_general | solution.py:120
  133.4 0.7 gather_fusion.1
  134.1 0.1 broadcast_select_fusion
  134.2 23.9 %all_to_all.10 = bf16[8,32,384]{2,1,0:T(8,128)(2,1)S(1)} all-to-all(bf16[8,32,384]{2,1,0:T(8,128)(2,1)S(1)} %broadcast_select_fusion), channel_id=1, replica_groups=mesh['seq'=8,'fsdp'=4] {'seq'}, dimensions={0} | all-to-all | bytes 393216 | tf_op jit(solution)/shard_map/all_to_all | solution.py:157
  158.1 0.7 copy.74
  (31 shorter events, 0.2 us)
Async XLA Ops:
  6.5 45.9 %copy-start = (bf16[2048,384]{1,0:T(8,128)(2,1)S(1)}, bf16[2048,384]{1,0:T(8,128)(2,1)}, u32[]{:S(2)}) copy-start(bf16[2048,384]{1,0:T(8,128)(2,1)} %param.17) | copy-start | bytes 4718596
  6.5 41.7 %copy-start.1 = (bf16[512,512]{1,0:T(8,128)(2,1)S(1)}, bf16[512,512]{1,0:T(8,128)(2,1)}, u32[]{:S(2)}) copy-start(bf16[512,512]{1,0:T(8,128)(2,1)} %param.19) | copy-start | bytes 1572868
  6.5 16.4 %all-to-all-start = ((bf16[8,32,512]{2,1,0:T(8,128)(2,1)}), bf16[8,32,512]{2,1,0:T(8,128)(2,1)}, u32[]{:S(2)}, u32[]{:S(2)}) async-start(bf16[8,32,512]{2,1,0:T(8,128)(2,1)} %bitcast.89), calls=%async_computation | async-start | bytes 524288 | tf_op jit(solution)/shard_map/all_to_all | solution.py:107
  14.0 38.5 %all-gather.5.cloned.1.call-start = ((), (), s32[]{:S(2)}) async-start(), calls=%async_computation.2 | async-start | bytes 1310720 | tf_op jit(solution)/shard_map/all_gather | solution.py:117
  14.0 8.9 %collective-permute-start = (bf16[512,512]{1,0:T(8,128)(2,1)}, bf16[512,512]{1,0:T(8,128)(2,1)S(1)}, u32[]{:S(2)}, u32[]{:S(2)}) collective-permute-start(bf16[512,512]{1,0:T(8,128)(2,1)} %param.19), channel_id=1, source_target_pairs={{0,1},{1,2},{2,3},{3,0},{4,5},{5,6},{6,7},{7,4},{8,9},{9,10},{10,1... | collective-permute-start | bytes 1572872 | tf_op jit(solution)/shard_map/ppermute | solution.py:14
  22.9 8.6 %collective-permute-start.1 = (bf16[512,512]{1,0:T(8,128)(2,1)S(1)}, bf16[512,512]{1,0:T(8,128)(2,1)S(1)}, u32[]{:S(2)}, u32[]{:S(2)}) collective-permute-start(bf16[512,512]{1,0:T(8,128)(2,1)S(1)} %collective-permute-done), channel_id=1, source_target_pairs={{0,1},{1,2},{2,3},{3,0},{4,5},{5,6},{6,7},{7,4},{8,9},{9,10},{10,1... | collective-permute-start | bytes 1572872 | tf_op jit(solution)/shard_map/ppermute | solution.py:14
  25.3 102.1 %all-gather.7.cloned.1.call-start = ((), (), s32[]{:S(2)}) async-start(), calls=%async_computation.3 | async-start | bytes 3538944 | tf_op jit(solution)/shard_map/all_gather | solution.py:28
  31.5 14.2 %collective-permute-start.2 = (bf16[512,512]{1,0:T(8,128)(2,1)S(1)}, bf16[512,512]{1,0:T(8,128)(2,1)S(1)}, u32[]{:S(2)}, u32[]{:S(2)}) collective-permute-start(bf16[512,512]{1,0:T(8,128)(2,1)S(1)} %collective-permute-done.1), channel_id=1, source_target_pairs={{0,1},{1,2},{2,3},{3,0},{4,5},{5,6},{6,7},{7,4},{8,9},{9,10},{10,1... | collective-permute-start | bytes 1572872 | tf_op jit(solution)/shard_map/ppermute | solution.py:14
  51.6 9.4 %copy-start.3 = (bf16[2048,6]{0,1:T(8,128)(2,1)S(1)}, bf16[2048,6]{0,1:T(8,128)(2,1)}, u32[]{:S(2)}) copy-start(bf16[2048,6]{0,1:T(8,128)(2,1)} %param.20) | copy-start | bytes 73732
  51.6 9.4 %copy-start.6 = (f32[6]{0:T(128)S(1)}, f32[6]{0:T(128)}, u32[]{:S(2)}) copy-start(f32[6]{0:T(128)} %param.23) | copy-start | bytes 76
  52.4 8.5 %copy-start.2 = (bf16[256,2048]{1,0:T(8,128)(2,1)S(1)}, bf16[256,2048]{1,0:T(8,128)(2,1)}, u32[]{:S(2)}) copy-start(bf16[256,2048]{1,0:T(8,128)(2,1)} %all-gather.5.cloned.1.call-done) | copy-start | bytes 3145732
  57.1 7.5 %collective-permute-start.3 = (bf16[3,896]{1,0:T(4,128)(2,1)S(1)}, bf16[3,896]{1,0:T(4,128)(2,1)S(1)}, u32[]{:S(2)}, u32[]{:S(2)}) collective-permute-start(bf16[3,896]{1,0:T(4,128)(2,1)S(1)} %pad_maximum_fusion), channel_id=1, source_target_pairs={{0,4},{4,8},{8,12},{12,16},{16,20},{20,24},{24,28},{1,5},{5,9},{9,... | collective-permute-start | bytes 16136 | tf_op jit(solution)/shard_map/ppermute | solution.py:23
  63.6 3.2 %copy-start.4 = (f32[1,6,2,128]{3,1,2,0:T(8,128)}, f32[1,6,2,128]{3,1,2,0:T(8,128)S(1)}, u32[]{:S(2)}) copy-start(f32[1,6,2,128]{3,1,2,0:T(8,128)S(1)} %copy.58) | copy-start | bytes 18436
  128.0 6.2 %copy-start.5 = (pred[8]{0:T(512)(128)(4,1)S(1)}, pred[8]{0:T(512)(128)(4,1)}, u32[]{:S(2)}) copy-start(pred[8]{0:T(512)(128)(4,1)} %get-tuple-element.68) | copy-start | bytes 28
Sparse Core Ops, SparseCore 0:
  25.5 21.1 all-gather.4
  67.0 60.4 all-gather.6
